TPU v7x, 32 devices: a whole 2x2x4 slice. The times are simulated.
32 devices in a mesh: dp: 4 (over x, core), seq: 8 (over z, y).
Axes of the slice: x: 2, y: 2, z: 4, core: 2. Of those that a mesh axis runs over, the one named last changes fastest.
Arguments:
- inputs: bfloat16 [2, 4, 1024, 768], P(None, 'dp', 'seq'), may hold values from -6 to 6
- cotangent: bfloat16 [2, 4, 1024, 768], P(None, 'dp', 'seq'), may hold values from -6 to 6
- bounds: int32 [2, 4, 2, 2], P(None, 'dp'), may hold values from 0 to 1024, as said below
- ln1_gain: bfloat16 [768], P(('dp', 'seq')), may hold values from 0.5 to 1.5
- ln1_bias: bfloat16 [768], P(('dp', 'seq')), may hold values from -1 to 1
- w_qkv: bfloat16 [768, 2304], P(('dp', 'seq')), may hold values from -0.21875 to 0.21875
- b_query: bfloat16 [768], P(('dp', 'seq')), may hold values from -1.5 to 1.5
- b_value: bfloat16 [768], P(('dp', 'seq')), may hold values from -1.5 to 1.5
- w_out: bfloat16 [768, 768], P(('dp', 'seq')), may hold values from -1.25 to 1.25
- b_out: bfloat16 [768], P(('dp', 'seq')), may hold values from -1.5 to 1.5
- ln2_gain: bfloat16 [768], P(('dp', 'seq')), may hold values from 0.5 to 1.5
- ln2_bias: bfloat16 [768], P(('dp', 'seq')), may hold values from -1 to 1
- w_up: bfloat16 [768, 3072], P(('dp', 'seq')), may hold values from -0.21875 to 0.21875
- b_up: bfloat16 [3072], P(('dp', 'seq')), may hold values from -1.5 to 1.5
- w_down: bfloat16 [3072, 768], P(('dp', 'seq')), may hold values from -0.109375 to 0.109375
- b_down: bfloat16 [768], P(('dp', 'seq')), may hold values from -1.5 to 1.5
Outputs:
- outputs: bfloat16 [2, 4, 1024, 768], P(None, 'dp', 'seq')
- input_grad: bfloat16 [2, 4, 1024, 768], P(None, 'dp', 'seq')
- grad_ln1_gain: float32 [768], P(('dp', 'seq'))
- grad_ln1_bias: float32 [768], P(('dp', 'seq'))
- grad_w_qkv: float32 [768, 2304], P(('dp', 'seq'))
- grad_b_query: float32 [768], P(('dp', 'seq'))
- grad_b_value: float32 [768], P(('dp', 'seq'))
- grad_w_out: float32 [768, 768], P(('dp', 'seq'))
- grad_b_out: float32 [768], P(('dp', 'seq'))
- grad_ln2_gain: float32 [768], P(('dp', 'seq'))
- grad_ln2_bias: float32 [768], P(('dp', 'seq'))
- grad_w_up: float32 [768, 3072], P(('dp', 'seq'))
- grad_b_up: float32 [3072], P(('dp', 'seq'))
- grad_w_down: float32 [3072, 768], P(('dp', 'seq'))
- grad_b_down: float32 [768], P(('dp', 'seq'))
Inputs may be any that keep to these rules, and one draw needn't show every extreme that they name: `bounds`: for each sequence, 2 picture pieces [start, end) of exactly 256 rows each, in increasing order and not intersecting.
All inputs are finite; a program needn't handle non-finite values.
Results may differ from a plain program's by a relative error of at most 0.02.
Values may be sent and summed in bfloat16 or wider, within the bound.
No kernel may reach another device: no remote copies, remote signals or barrier semaphores. Data moves between devices by JAX's collectives and lax.ppermute only.
A program may use at most 256 MiB of HBM per device.

v0:
```python
from functools import partial
import jax
import jax.numpy as jnp
from jax import lax
from jax.sharding import PartitionSpec as P

HEADS = 12
HEAD = 64
EPSILON = 1e-05


def layer_norm(values, ln_gain, ln_shift):
    center = jnp.mean(values, axis=-1, keepdims=True)
    centered = values - center
    spread = jnp.mean(centered * centered, axis=-1, keepdims=True)
    return centered * lax.rsqrt(spread + EPSILON) * ln_gain + ln_shift


def piece_label(positions, bounds):
    inside = (positions[:, None] >= bounds[None, :, 0]) & (positions[:, None] < bounds[None, :, 1])
    labels = jnp.arange(1, bounds.shape[0] + 1, dtype=jnp.int32)
    return jnp.sum(jnp.where(inside, labels[None, :], 0), axis=1) - 1


def allowed_mask(query_pos, key_pos, bounds):
    query_label = piece_label(query_pos, bounds)
    key_label = piece_label(key_pos, bounds)
    causal = key_pos[None, :] <= query_pos[:, None]
    same_piece = (query_label[:, None] == key_label[None, :]) & (query_label[:, None] >= 0)
    return causal | same_piece


def outer_rows(left, right):
    return lax.dot_general(
        left, right, (((0,), (0,)), ((), ())), preferred_element_type=jnp.float32
    )


def times_transposed(left, right):
    return lax.dot_general(
        left, right, (((1,), (1,)), ((), ())), preferred_element_type=jnp.float32
    )


def key_step():
    return 512


def masked_weights(query_heads, key_heads, query_pos, key_pos, bounds):
    factor = query_heads.shape[2] ** (-0.5)
    scores = (
        jnp.einsum("rhd,khd->hrk", query_heads, key_heads, preferred_element_type=jnp.float32)
        * factor
    )
    allowed = allowed_mask(query_pos, key_pos, bounds)
    return jnp.where(allowed[None], jnp.exp(scores), 0.0)


def forward_fold(query_heads, query_pos, bounds):
    head_count = query_heads.shape[1]

    def fold_keys(carry, piece, first_row):
        key_piece, value_piece = piece
        piece_len = key_piece.shape[0]
        step_len = key_step()

        def inner_step(block_idx, partial_sums):
            weighted, totals = partial_sums
            offset = block_idx * step_len
            key_heads = lax.dynamic_slice_in_dim(key_piece, offset, step_len, 0).reshape(
                step_len, head_count, -1
            )
            value_heads = lax.dynamic_slice_in_dim(value_piece, offset, step_len, 0).reshape(
                step_len, head_count, -1
            )
            key_pos = offset + jnp.arange(step_len, dtype=jnp.int32)
            weights = masked_weights(query_heads, key_heads, query_pos, key_pos, bounds)
            weighted = weighted + jnp.einsum(
                "hrk,khd->rhd",
                weights.astype(jnp.bfloat16),
                value_heads,
                preferred_element_type=jnp.float32,
            )
            return (weighted, totals + jnp.sum(weights, axis=-1))

        return lax.fori_loop(0, piece_len // step_len, inner_step, carry)

    return fold_keys


def backward_fold(query_heads, query_pos, bounds, grad_heads, delta):
    head_count = query_heads.shape[1]
    factor = query_heads.shape[2] ** (-0.5)

    def fold_grads(carry, piece, first_row):
        key_piece, value_piece = piece
        piece_len = key_piece.shape[0]
        step_len = key_step()

        def inner_step(block_idx, partial_sums):
            query_grad, key_grad, value_grad = partial_sums
            offset = block_idx * step_len
            key_heads = lax.dynamic_slice_in_dim(key_piece, offset, step_len, 0).reshape(
                step_len, head_count, -1
            )
            value_heads = lax.dynamic_slice_in_dim(value_piece, offset, step_len, 0).reshape(
                step_len, head_count, -1
            )
            key_pos = offset + jnp.arange(step_len, dtype=jnp.int32)
            weights = masked_weights(query_heads, key_heads, query_pos, key_pos, bounds)
            products = jnp.einsum(
                "rhd,khd->hrk", grad_heads, value_heads, preferred_element_type=jnp.float32
            )
            score_grad = (weights * (products - delta[:, :, None])).astype(jnp.bfloat16)
            query_grad = (
                query_grad
                + jnp.einsum(
                    "hrk,khd->rhd", score_grad, key_heads, preferred_element_type=jnp.float32
                )
                * factor
            )
            key_rows = (
                jnp.einsum(
                    "hrk,rhd->khd", score_grad, query_heads, preferred_element_type=jnp.float32
                )
                * factor
            ).reshape(step_len, -1)
            value_rows = jnp.einsum(
                "hrk,rhd->khd",
                weights.astype(jnp.bfloat16),
                grad_heads,
                preferred_element_type=jnp.float32,
            ).reshape(step_len, -1)
            key_grad = lax.dynamic_update_slice_in_dim(key_grad, key_rows, offset, 0)
            value_grad = lax.dynamic_update_slice_in_dim(value_grad, value_rows, offset, 0)
            return (query_grad, key_grad, value_grad)

        return lax.fori_loop(0, piece_len // step_len, inner_step, carry)

    return fold_grads


def body(
    inputs,
    cotangent,
    bounds,
    ln1_gain,
    ln1_bias,
    w_qkv,
    b_query,
    b_value,
    w_out,
    b_out,
    ln2_gain,
    ln2_bias,
    w_up,
    b_up,
    w_down,
    b_down,
):
    shards = (
        ln1_gain,
        ln1_bias,
        w_qkv,
        b_query,
        b_value,
        w_out,
        b_out,
        ln2_gain,
        ln2_bias,
        w_up,
        b_up,
        w_down,
        b_down,
    )
    micro_count = inputs.shape[0]
    row_count = inputs.shape[2]
    width = inputs.shape[3]
    total_len = row_count * lax.axis_size("seq")
    query_pos = lax.axis_index("seq") * row_count + jnp.arange(row_count, dtype=jnp.int32)
    grad_sums = [None] * 13
    outputs_list = []
    input_grads = []
    for micro_idx in range(micro_count):
        gathered = (
            lax.all_gather(shards[0], ("dp", "seq"), axis=0, tiled=True),
            lax.all_gather(shards[1], ("dp", "seq"), axis=0, tiled=True),
            lax.all_gather(shards[2], ("dp", "seq"), axis=0, tiled=True),
            lax.all_gather(shards[3], ("dp", "seq"), axis=0, tiled=True),
            lax.all_gather(shards[4], ("dp", "seq"), axis=0, tiled=True),
            lax.all_gather(shards[5], ("dp", "seq"), axis=0, tiled=True),
            lax.all_gather(shards[6], ("dp", "seq"), axis=0, tiled=True),
            lax.all_gather(shards[7], ("dp", "seq"), axis=0, tiled=True),
            lax.all_gather(shards[8], ("dp", "seq"), axis=0, tiled=True),
            lax.all_gather(shards[9], ("dp", "seq"), axis=0, tiled=True),
            lax.all_gather(shards[10], ("dp", "seq"), axis=0, tiled=True),
            lax.all_gather(shards[11], ("dp", "seq"), axis=0, tiled=True),
            lax.all_gather(shards[12], ("dp", "seq"), axis=0, tiled=True),
        )
        (
            gain_one,
            shift_one,
            proj_qkv,
            bias_query,
            bias_value,
            proj_out,
            bias_out,
            gain_two,
            shift_two,
            proj_up,
            bias_up,
            proj_down,
            bias_down,
        ) = gathered
        seq_bounds = bounds[micro_idx, 0]
        seq_in = inputs[micro_idx, 0].astype(jnp.float32)
        normed_f, norm_one_back = jax.vjp(
            layer_norm, seq_in, gain_one.astype(jnp.float32), shift_one.astype(jnp.float32)
        )
        normed = normed_f.astype(jnp.bfloat16)
        projected = jnp.dot(normed, proj_qkv, preferred_element_type=jnp.float32)
        queries = (projected[:, :width] + bias_query.astype(jnp.float32)).astype(jnp.bfloat16)
        keys_now = projected[:, width : 2 * width].astype(jnp.bfloat16)
        values_now = (projected[:, 2 * width :] + bias_value.astype(jnp.float32)).astype(
            jnp.bfloat16
        )
        query_heads = queries.reshape(row_count, HEADS, HEAD)
        start_sums = (
            jnp.zeros((row_count, HEADS, HEAD), jnp.float32),
            jnp.zeros((HEADS, row_count), jnp.float32),
        )
        fold_keys = forward_fold(query_heads, query_pos, seq_bounds)
        weighted, totals = fold_keys(
            start_sums,
            (
                lax.all_gather(keys_now, "seq", axis=0, tiled=True),
                lax.all_gather(values_now, "seq", axis=0, tiled=True),
            ),
            jnp.int32(0),
        )
        attended = weighted / totals.T[:, :, None]
        attended_b = attended.reshape(row_count, width).astype(jnp.bfloat16)
        branch = jnp.dot(
            attended_b, proj_out, preferred_element_type=jnp.float32
        ) + bias_out.astype(jnp.float32)
        middle = seq_in + branch
        normed_two_f, norm_two_back = jax.vjp(
            layer_norm, middle, gain_two.astype(jnp.float32), shift_two.astype(jnp.float32)
        )
        normed_two = normed_two_f.astype(jnp.bfloat16)
        hidden = jnp.dot(normed_two, proj_up, preferred_element_type=jnp.float32) + bias_up.astype(
            jnp.float32
        )
        activated_f, gelu_back = jax.vjp(partial(jax.nn.gelu, approximate=False), hidden)
        activated = activated_f.astype(jnp.bfloat16)
        mlp_out = jnp.dot(
            activated, proj_down, preferred_element_type=jnp.float32
        ) + bias_down.astype(jnp.float32)
        outputs_list.append((middle + mlp_out).astype(jnp.bfloat16))
        qkv_back, out_back, up_back, down_back = (
            lax.all_gather(w_qkv, ("dp", "seq"), axis=0, tiled=True),
            lax.all_gather(w_out, ("dp", "seq"), axis=0, tiled=True),
            lax.all_gather(w_up, ("dp", "seq"), axis=0, tiled=True),
            lax.all_gather(w_down, ("dp", "seq"), axis=0, tiled=True),
        )
        out_grad = cotangent[micro_idx, 0]
        out_grad_f = out_grad.astype(jnp.float32)
        grad_down = outer_rows(activated, out_grad)
        grad_bias_down = jnp.sum(out_grad_f, axis=0)
        act_grad = times_transposed(out_grad, down_back)
        (hidden_grad,) = gelu_back(act_grad)
        hidden_grad_b = hidden_grad.astype(jnp.bfloat16)
        grad_up = outer_rows(normed_two, hidden_grad_b)
        grad_bias_up = jnp.sum(hidden_grad_b.astype(jnp.float32), axis=0)
        normed_two_grad = times_transposed(hidden_grad_b, up_back)
        middle_ln_grad, grad_gain_two, grad_shift_two = norm_two_back(normed_two_grad)
        middle_grad = out_grad_f + middle_ln_grad
        branch_grad = middle_grad.astype(jnp.bfloat16)
        grad_out = outer_rows(attended_b, branch_grad)
        grad_bias_out = jnp.sum(branch_grad.astype(jnp.float32), axis=0)
        attended_grad = times_transposed(branch_grad, out_back).astype(jnp.bfloat16)
        attended_grad_f = attended_grad.astype(jnp.float32).reshape(row_count, HEADS, HEAD)
        delta = jnp.sum(attended_grad_f * attended, axis=-1).T / totals
        grad_heads = (attended_grad_f / totals.T[:, :, None]).astype(jnp.bfloat16)
        start_grads = (
            jnp.zeros((row_count, HEADS, HEAD), jnp.float32),
            jnp.zeros((total_len, width), jnp.float32),
            jnp.zeros((total_len, width), jnp.float32),
        )
        fold_grads = backward_fold(query_heads, query_pos, seq_bounds, grad_heads, delta)
        folded = fold_grads(
            start_grads,
            (
                lax.all_gather(keys_now, "seq", axis=0, tiled=True),
                lax.all_gather(values_now, "seq", axis=0, tiled=True),
            ),
            jnp.int32(0),
        )
        query_grad = folded[0]
        key_own, value_own = (
            lax.psum_scatter(
                folded[1].astype(jnp.bfloat16), "seq", scatter_dimension=0, tiled=True
            ).astype(jnp.float32),
            lax.psum_scatter(
                folded[2].astype(jnp.bfloat16), "seq", scatter_dimension=0, tiled=True
            ).astype(jnp.float32),
        )
        query_grad_b = query_grad.reshape(row_count, width).astype(jnp.bfloat16)
        key_grad_b = key_own.astype(jnp.bfloat16)
        value_grad_b = value_own.astype(jnp.bfloat16)
        proj_grad = jnp.concatenate([query_grad_b, key_grad_b, value_grad_b], axis=1)
        grad_qkv = outer_rows(normed, proj_grad)
        grad_bias_query = jnp.sum(query_grad_b.astype(jnp.float32), axis=0)
        grad_bias_value = jnp.sum(value_grad_b.astype(jnp.float32), axis=0)
        normed_grad = times_transposed(proj_grad, qkv_back)
        input_ln_grad, grad_gain_one, grad_shift_one = norm_one_back(normed_grad)
        input_grads.append((middle_grad + input_ln_grad).astype(jnp.bfloat16))
        current = (
            grad_gain_one,
            grad_shift_one,
            grad_qkv,
            grad_bias_query,
            grad_bias_value,
            grad_out,
            grad_bias_out,
            grad_gain_two,
            grad_shift_two,
            grad_up,
            grad_bias_up,
            grad_down,
            grad_bias_down,
        )
        grad_sums = [
            fresh if before is None else before + fresh for before, fresh in zip(grad_sums, current)
        ]
    reduced = lax.psum_scatter(tuple(grad_sums), ("dp", "seq"), scatter_dimension=0, tiled=True)
    return (jnp.stack(outputs_list)[:, None], jnp.stack(input_grads)[:, None]) + tuple(reduced)


def solution(mesh):
    return jax.shard_map(
        body,
        mesh=mesh,
        in_specs=(
            P(None, "dp", "seq", None),
            P(None, "dp", "seq", None),
            P(None, "dp", None, None),
            P(("dp", "seq")),
            P(("dp", "seq")),
            P(("dp", "seq"), None),
            P(("dp", "seq")),
            P(("dp", "seq")),
            P(("dp", "seq"), None),
            P(("dp", "seq")),
            P(("dp", "seq")),
            P(("dp", "seq")),
            P(("dp", "seq"), None),
            P(("dp", "seq")),
            P(("dp", "seq"), None),
            P(("dp", "seq")),
        ),
        out_specs=(
            P(None, "dp", "seq", None),
            P(None, "dp", "seq", None),
            P(("dp", "seq")),
            P(("dp", "seq")),
            P(("dp", "seq"), None),
            P(("dp", "seq")),
            P(("dp", "seq")),
            P(("dp", "seq"), None),
            P(("dp", "seq")),
            P(("dp", "seq")),
            P(("dp", "seq")),
            P(("dp", "seq"), None),
            P(("dp", "seq")),
            P(("dp", "seq"), None),
            P(("dp", "seq")),
        ),
        check_vma=False,
    )
```

profile of v0, /device:TPU:0, one launch (start us, length us, event | category | flops | bytes accessed | tf_op | source)
XLA Modules:
  0.0 1279.3 jit_solution(13797985035123870307)
XLA Ops:
  15.5 42.8 %all-reduce.19 = (bf16[768]{0:T(1024)(128)(2,1)S(1)}, bf16[768]{0:T(1024)(128)(2,1)S(1)}, bf16[768]{0:T(1024)(128)(2,1)S(1)}, bf16[768]{0:T(1024)(128)(2,1)S(1)}...) all-reduce(bf16[768]{0:T(1024)(128)(2,1)S(1)} %dynamic-update-slice, ...), channel_id=1, replica_groups=mesh['dp'=4,'seq'=8] {'dp','seq'}, use_global_device_ids=true, to_apply=%add.1 | all-reduce | flops 9216 | bytes 36864
  61.4 12.4 all-gather.9.cloned.1.call-done
  87.0 34.6 %all-gather.21.cloned.1.call-done = bf16[1024,768]{1,0:T(8,128)(2,1)} async-done(((bf16[128,768]{1,0:T(8,128)(2,1)}), bf16[1024,768]{1,0:T(8,128)(2,1)}) %all-gather.21.cloned.1.call-update) | async-done | bytes 1572880 | tf_op jit(solution)/shard_map/all_gather | solution.py:237
  124.3 42.7 %all-gather.23.cloned.1.call-done = bf16[1024,768]{1,0:T(8,128)(2,1)} async-done(((bf16[128,768]{1,0:T(8,128)(2,1)}), bf16[1024,768]{1,0:T(8,128)(2,1)}) %all-gather.23.cloned.1.call-update) | async-done | bytes 1572880 | tf_op jit(solution)/shard_map/all_gather | solution.py:236
  169.6 15.7 %while.81 = (s32[]{:T(128)}, f32[128,12,64]{0,2,1:T(8,128)}, f32[12,128]{1,0:T(8,128)S(1)}, bf16[1024,768]{0,1:T(8,128)(2,1)}, s32[2,2]{0,1:T(2,128)}, /*index=5...) while((s32[]{:T(128)}, f32[128,12,64]{0,2,1:T(8,128)}, ...), condition=%wide.region_15.16_spmd.clone, body=%wide.region_11.0_spmd.clone.sunk | while | flops 206512768 | bytes 12520018 | solution.py:86
  186.4 35.8 %all-gather.15.cloned.1.call-done = bf16[768,768]{1,0:T(8,128)(2,1)} async-done(((bf16[24,768]{1,0:T(8,128)(2,1)}), bf16[768,768]{1,0:T(8,128)(2,1)}) %all-gather.15.cloned.1.call-update) | async-done | bytes 1179664 | tf_op jit(solution)/shard_map/all_gather | solution.py:191
  225.4 42.5 %all-gather.11.cloned.1.call-done = bf16[1024,768]{1,0:T(8,128)(2,1)} async-done(((bf16[128,768]{1,0:T(8,128)(2,1)}), bf16[1024,768]{1,0:T(8,128)(2,1)}) %all-gather.11.cloned.1.call-update) | async-done | bytes 1572880 | tf_op jit(solution)/shard_map/all_gather | solution.py:237
  270.5 42.0 %all-gather.13.cloned.1.call-done = bf16[1024,768]{1,0:T(8,128)(2,1)} async-done(((bf16[128,768]{1,0:T(8,128)(2,1)}), bf16[1024,768]{1,0:T(8,128)(2,1)}) %all-gather.13.cloned.1.call-update) | async-done | bytes 1572880 | tf_op jit(solution)/shard_map/all_gather | solution.py:236
  315.2 14.2 %while.80 = (s32[]{:T(128)}, f32[128,12,64]{0,2,1:T(8,128)}, f32[12,128]{1,0:T(8,128)S(1)}, bf16[1024,768]{0,1:T(8,128)(2,1)}, s32[2,2]{0,1:T(2,128)}, /*index=5...) while((s32[]{:T(128)}, f32[128,12,64]{0,2,1:T(8,128)}, ...), condition=%wide.region_6.7_spmd.clone, body=%wide.region_2.6_spmd.clone.sunk | while | flops 206512768 | bytes 12233242 | solution.py:86
  332.6 44.8 %all-gather.17.cloned.1.call-done = bf16[768,3072]{1,0:T(8,128)(2,1)} async-done(((bf16[24,3072]{1,0:T(8,128)(2,1)}), bf16[768,3072]{1,0:T(8,128)(2,1)}) %all-gather.17.cloned.1.call-update) | async-done | bytes 4718608 | tf_op jit(solution)/shard_map/all_gather | solution.py:195
  377.5 8.7 multiply_convert_fusion
  386.2 6.4 multiply_convert_fusion.1
  392.6 49.6 %all-gather.19.cloned.1.call-done = bf16[3072,768]{1,0:T(8,128)(2,1)} async-done(((bf16[96,768]{1,0:T(8,128)(2,1)}), bf16[3072,768]{1,0:T(8,128)(2,1)}) %all-gather.19.cloned.1.call-update) | async-done | bytes 4718608 | tf_op jit(solution)/shard_map/all_gather | solution.py:197
  442.2 5.8 convert_reduce_fusion
  462.0 28.4 %while.83 = (s32[]{:T(128)}, f32[128,12,64]{0,2,1:T(8,128)}, bf16[1024,768]{0,1:T(8,128)(2,1)}, bf16[1024,768]{0,1:T(8,128)(2,1)}, bf16[1024,768]{0,1:T(8,128)(2...) while((s32[]{:T(128)}, f32[128,12,64]{0,2,1:T(8,128)}, ...), condition=%wide.region_35.36_spmd.clone, body=%wide.region_32.35_spmd.clone.sunk | while | flops 510958720 | bytes 62874448 | solution.py:138
  483.0 2.9 fusion.321
  499.9 28.7 %while.82 = (s32[]{:T(128)}, f32[128,12,64]{0,2,1:T(8,128)}, bf16[1024,768]{0,1:T(8,128)(2,1)}, bf16[1024,768]{0,1:T(8,128)(2,1)}, bf16[1024,768]{0,1:T(8,128)(2...) while((s32[]{:T(128)}, f32[128,12,64]{0,2,1:T(8,128)}, ...), condition=%wide.region_24.25_spmd.clone, body=%wide.region_21.24_spmd.clone.sunk | while | flops 510958720 | bytes 61301528 | solution.py:138
  521.1 2.9 fusion.305
  539.5 17.6 %reduce-scatter.31.cloned.1.call-done = bf16[128,768]{1,0:T(8,128)(2,1)} async-done(((bf16[1024,768]{1,0:T(8,128)(2,1)}), bf16[128,768]{1,0:T(8,128)(2,1)}) %reduce-scatter.31.cloned.1.call-update) | async-done | bytes 196624
  558.1 66.5 %reduce-scatter.29.cloned.1.call-done = bf16[128,768]{1,0:T(8,128)(2,1)} async-done(((bf16[1024,768]{1,0:T(8,128)(2,1)}), bf16[128,768]{1,0:T(8,128)(2,1)}) %reduce-scatter.29.cloned.1.call-update) | async-done | bytes 196624
  625.7 66.7 %reduce-scatter.27.cloned.1.call-done = bf16[128,768]{1,0:T(8,128)(2,1)} async-done(((bf16[1024,768]{1,0:T(8,128)(2,1)}), bf16[128,768]{1,0:T(8,128)(2,1)}) %reduce-scatter.27.cloned.1.call-update) | async-done | bytes 196624
  693.5 66.6 %reduce-scatter.25.cloned.1.call-done = bf16[128,768]{1,0:T(8,128)(2,1)} async-done(((bf16[1024,768]{1,0:T(8,128)(2,1)}), bf16[128,768]{1,0:T(8,128)(2,1)}) %reduce-scatter.25.cloned.1.call-update) | async-done | bytes 196624
  762.6 4.2 convolution_add_fusion
  769.6 5.2 convolution_add_fusion.2
  777.5 5.1 convolution_add_fusion.1
  792.3 3.2 fusion.88
  795.6 3.3 fusion.89
  803.5 40.7 %all-reduce.18 = (f32[768]{0:T(1024)S(1)}, f32[768]{0:T(1024)S(1)}, f32[768]{0:T(1024)S(1)}, f32[768]{0:T(1024)S(1)}, f32[768]{0:T(1024)S(1)}, /*index=5*/f32[76...) all-reduce(f32[768]{0:T(1024)S(1)} %add.789, ...), channel_id=6, replica_groups=mesh['dp'=4,'seq'=8] {'dp','seq'}, use_global_device_ids=true, to_apply=%region_42.43.clone | all-reduce | flops 9216 | bytes 73728
  850.7 14.1 %reduce-scatter.19.cloned.1.call-done = f32[24,768]{1,0:T(8,128)} async-done(((f32[768,768]{1,0:T(8,128)}), f32[24,768]{1,0:T(8,128)}) %reduce-scatter.19.cloned.1.call-update) | async-done | bytes 73744 | tf_op jit(solution)/shard_map/reduce_scatter | solution.py:336
  864.9 124.7 %reduce-scatter.17.cloned.1.call-done = f32[24,2304]{1,0:T(8,128)} async-done(((f32[768,2304]{1,0:T(8,128)}), f32[24,2304]{1,0:T(8,128)}) %reduce-scatter.17.cloned.1.call-update) | async-done | bytes 221200 | tf_op jit(solution)/shard_map/reduce_scatter | solution.py:336
  989.6 141.5 %reduce-scatter.21.cloned.1.call-done = f32[24,3072]{1,0:T(8,128)} async-done(((f32[768,3072]{1,0:T(8,128)}), f32[24,3072]{1,0:T(8,128)}) %reduce-scatter.21.cloned.1.call-update) | async-done | bytes 294928 | tf_op jit(solution)/shard_map/reduce_scatter | solution.py:336
  1131.1 141.5 %reduce-scatter.23.cloned.1.call-done = f32[96,768]{1,0:T(8,128)} async-done(((f32[3072,768]{1,0:T(8,128)}), f32[96,768]{1,0:T(8,128)}) %reduce-scatter.23.cloned.1.call-update) | async-done | bytes 294928 | tf_op jit(solution)/shard_map/reduce_scatter | solution.py:336
  (567 shorter events, 187.9 us)
Async XLA Ops:
  7.2 66.6 %all-gather.9.cloned.1.call-start = ((), (), s32[]{:S(2)}) async-start(), calls=%async_computation.8 | async-start | bytes 3649536 | tf_op jit(solution)/shard_map/all_gather | solution.py:188
  7.9 113.7 %all-gather.21.cloned.1.call-start = ((), (), s32[]{:S(2)}) async-start(), calls=%async_computation.14 | async-start | bytes 1769472 | tf_op jit(solution)/shard_map/all_gather | solution.py:237
  78.5 88.5 %all-gather.23.cloned.1.call-start = ((), (), s32[]{:S(2)}) async-start(), calls=%async_computation.15 | async-start | bytes 1769472 | tf_op jit(solution)/shard_map/all_gather | solution.py:236
  79.3 142.9 %all-gather.15.cloned.1.call-start = ((), (), s32[]{:S(2)}) async-start(), calls=%async_computation.11 | async-start | bytes 1216512 | tf_op jit(solution)/shard_map/all_gather | solution.py:191
  79.9 188.1 %all-gather.11.cloned.1.call-start = ((), (), s32[]{:S(2)}) async-start(), calls=%async_computation.9 | async-start | bytes 1769472 | tf_op jit(solution)/shard_map/all_gather | solution.py:237
  80.4 232.1 %all-gather.13.cloned.1.call-start = ((), (), s32[]{:S(2)}) async-start(), calls=%async_computation.10 | async-start | bytes 1769472 | tf_op jit(solution)/shard_map/all_gather | solution.py:236
  81.2 296.2 %all-gather.17.cloned.1.call-start = ((), (), s32[]{:S(2)}) async-start(), calls=%async_computation.12 | async-start | bytes 4866048 | tf_op jit(solution)/shard_map/all_gather | solution.py:195
  82.0 360.3 %all-gather.19.cloned.1.call-start = ((), (), s32[]{:S(2)}) async-start(), calls=%async_computation.13 | async-start | bytes 4866048 | tf_op jit(solution)/shard_map/all_gather | solution.py:197
  82.7 474.3 %reduce-scatter.31.cloned.1.call-start = ((), (), s32[]{:S(2)}) async-start(), calls=%async_computation.23 | async-start | bytes 1769472
  185.2 85.3 %copy-start.4 = (bf16[128,12,64]{0,2,1:T(8,128)(2,1)}, bf16[128,12,64]{0,2,1:T(8,128)(2,1)S(1)}, u32[]{:S(2)}) copy-start(bf16[128,12,64]{0,2,1:T(8,128)(2,1)S(1)} %get-tuple-element.2051) | copy-start | bytes 589828
  186.4 84.2 %copy-start.52 = (bf16[128,12,64]{0,2,1:T(8,128)(2,1)}, bf16[128,12,64]{0,2,1:T(8,128)(2,1)S(1)}, u32[]{:S(2)}) copy-start(bf16[128,12,64]{0,2,1:T(8,128)(2,1)S(1)} %fusion.137) | copy-start | bytes 589828
  330.5 55.6 %copy-start.56 = (bf16[128,12,64]{0,2,1:T(8,128)(2,1)}, bf16[128,12,64]{0,2,1:T(8,128)(2,1)S(1)}, u32[]{:S(2)}) copy-start(bf16[128,12,64]{0,2,1:T(8,128)(2,1)S(1)} %fusion.136) | copy-start | bytes 589828
  332.4 123.2 %copy-start.16 = (f32[128,768]{1,0:T(8,128)}, f32[128,768]{1,0:T(8,128)S(1)}, u32[]{:S(2)}) copy-start(f32[128,768]{1,0:T(8,128)S(1)} %get-tuple-element.1584) | copy-start | bytes 1179652
  332.4 123.2 %copy-start.92 = (f32[128]{0:T(128)}, f32[128]{0:T(128)S(1)}, u32[]{:S(2)}) copy-start(f32[128]{0:T(128)S(1)} %broadcast_multiply_fusion.2) | copy-start | bytes 1540
  332.6 123.0 %copy-start.106 = (f32[128]{0:T(128)}, f32[128]{0:T(128)S(1)}, u32[]{:S(2)}) copy-start(f32[128]{0:T(128)S(1)} %fusion.145) | copy-start | bytes 1540
  332.6 122.9 %copy-start.104 = (f32[128]{0:T(128)}, f32[128]{0:T(128)S(1)}, u32[]{:S(2)}) copy-start(f32[128]{0:T(128)S(1)} %fusion.143) | copy-start | bytes 1540
  386.2 56.1 %copy-start.41 = (bf16[2,1,128,768]{3,2,1,0:T(8,128)(2,1)S(1)}, bf16[2,1,128,768]{3,2,1,0:T(8,128)(2,1)}, u32[]{:S(2)}) copy-start(bf16[2,1,128,768]{3,2,1,0:T(8,128)(2,1)} %param.25) | copy-start | bytes 1179652
  493.0 131.7 %reduce-scatter.29.cloned.1.call-start = ((), (), s32[]{:S(2)}) async-start(), calls=%async_computation.22 | async-start | bytes 1769472
  497.1 195.4 %reduce-scatter.27.cloned.1.call-start = ((), (), s32[]{:S(2)}) async-start(), calls=%async_computation.21 | async-start | bytes 1769472
  531.2 229.0 %reduce-scatter.25.cloned.1.call-start = ((), (), s32[]{:S(2)}) async-start(), calls=%async_computation.20 | async-start | bytes 1769472
  534.2 330.7 %reduce-scatter.19.cloned.1.call-start = ((), (), s32[]{:S(2)}) async-start(), calls=%async_computation.17 | async-start | bytes 2433024 | tf_op jit(solution)/shard_map/reduce_scatter | solution.py:336
  537.5 223.7 %copy-start.8 = (bf16[2,1,128,768]{3,2,1,0:T(8,128)(2,1)S(1)}, bf16[2,1,128,768]{3,2,1,0:T(8,128)(2,1)}, u32[]{:S(2)}) copy-start(bf16[2,1,128,768]{3,2,1,0:T(8,128)(2,1)} %param.24) | copy-start | bytes 1179652
  537.6 223.7 %copy-start.69 = (f32[768]{0:T(1024)S(1)}, f32[768]{0:T(1024)}, u32[]{:S(2)}) copy-start(f32[768]{0:T(1024)} %copy-done.68) | copy-start | bytes 9220
  537.6 223.7 %copy-start.74 = (f32[768]{0:T(1024)S(1)}, f32[768]{0:T(1024)}, u32[]{:S(2)}) copy-start(f32[768]{0:T(1024)} %copy-done.73) | copy-start | bytes 9220
  537.6 223.7 %copy-start.81 = (f32[128]{0:T(128)S(1)}, f32[128]{0:T(128)}, u32[]{:S(2)}) copy-start(f32[128]{0:T(128)} %copy-done.80) | copy-start | bytes 1540
  537.6 223.7 %copy-start.95 = (f32[128]{0:T(128)S(1)}, f32[128]{0:T(128)}, u32[]{:S(2)}) copy-start(f32[128]{0:T(128)} %copy-done.94) | copy-start | bytes 1540
  537.6 452.0 %reduce-scatter.17.cloned.1.call-start = ((), (), s32[]{:S(2)}) async-start(), calls=%async_computation.16 | async-start | bytes 7299072 | tf_op jit(solution)/shard_map/reduce_scatter | solution.py:336
  538.7 223.9 %copy-start.62 = (bf16[128,12,64]{0,2,1:T(8,128)(2,1)}, bf16[128,12,64]{0,2,1:T(8,128)(2,1)S(1)}, u32[]{:S(2)}) copy-start(bf16[128,12,64]{0,2,1:T(8,128)(2,1)S(1)} %get-tuple-element.1526) | copy-start | bytes 589828
  539.5 223.1 %copy-start.66 = (bf16[128,12,64]{0,2,1:T(8,128)(2,1)}, bf16[128,12,64]{0,2,1:T(8,128)(2,1)S(1)}, u32[]{:S(2)}) copy-start(bf16[128,12,64]{0,2,1:T(8,128)(2,1)S(1)} %get-tuple-element.1528) | copy-start | bytes 589828
  625.7 136.8 %copy-start.60 = (bf16[128,768]{0,1:T(8,128)(2,1)}, bf16[128,768]{0,1:T(8,128)(2,1)S(1)}, u32[]{:S(2)}) copy-start(bf16[128,768]{0,1:T(8,128)(2,1)S(1)} %copy.152) | copy-start | bytes 589828
  766.9 364.2 %reduce-scatter.21.cloned.1.call-start = ((), (), s32[]{:S(2)}) async-start(), calls=%async_computation.18 | async-start | bytes 9732096 | tf_op jit(solution)/shard_map/reduce_scatter | solution.py:336
  774.8 497.8 %reduce-scatter.23.cloned.1.call-start = ((), (), s32[]{:S(2)}) async-start(), calls=%async_computation.19 | async-start | bytes 9732096 | tf_op jit(solution)/shard_map/reduce_scatter | solution.py:336
  (124 other events, 784.3 us)
Sparse Core Ops, SparseCore 0:
  10.9 62.7 all-gather.8
  78.6 42.9 all-gather.20
  124.4 42.5 all-gather.22
  169.7 52.4 all-gather.14
  224.8 43.0 all-gather.10
  270.0 42.5 all-gather.12
  315.4 61.9 all-gather.16
  380.4 61.8 all-gather.18
  493.1 63.8 reduce-scatter.30
  560.3 64.2 reduce-scatter.28
  628.1 64.2 reduce-scatter.26
  695.7 64.3 reduce-scatter.24
  766.0 98.8 reduce-scatter.18
  871.0 118.5 reduce-scatter.16
  995.9 135.1 reduce-scatter.20
  1137.4 135.1 reduce-scatter.22
where the time goes:
time: 1290 us; the launch traced here: 1280 us
  waiting for transfers between devices  947 us (73%)
  matrix products  110 us (9%)
  local copies, waits for them, and re-layouts  94.1 us (7%)
  blocking collectives  83.5 us (6%)
  other arithmetic  26.8 us (2%)
  between operations  15.6 us (1%)
    reduce_scatter x4, waiting for transfers between devices, body(): lax.psum_scatter(tuple(grad_sums), ('dp', 'seq'), scatter_dimension=0, ti...  422 us
    unnamed x20, waiting for transfers between devices  221 us
    all_gather x2, waiting for transfers between devices, body(): lax.all_gather(keys_now, 'seq', axis=0, tiled=True)  84.7 us
    unnamed x2, blocking collectives  83.5 us
    all_gather x2, waiting for transfers between devices, body(): lax.all_gather(values_now, 'seq', axis=0, tiled=True)  77.2 us
    all_gather x1, waiting for transfers between devices, body(): lax.all_gather(shards[11], ('dp', 'seq'), axis=0, tiled=True)  49.6 us
    unnamed x241, local copies, waits for them, and re-layouts  47.1 us
    all_gather x1, waiting for transfers between devices, body(): lax.all_gather(shards[9], ('dp', 'seq'), axis=0, tiled=True)  44.8 us
  transfers between devices with their start and end apart: 16, of which 16 were waited for; matrix products, arithmetic and copies ran while one was open for 13% of the time, Pallas kernels for 0%

commit v1 on v0

--- a/solution.py
+++ b/solution.py
@@ -234,7 +234,10 @@
             start_sums,
             (
                 lax.all_gather(keys_now, "seq", axis=0, tiled=True),
-                lax.all_gather(values_now, "seq", axis=0, tiled=True),
+                jnp.concatenate(
+                    lax.all_to_all(jnp.stack([values_now] * lax.axis_size("seq")), "seq", 0, 0),
+                    axis=0,
+                ),
             ),
             jnp.int32(0),
         )

time: 1290 us -> 1270 us (0.984)
  waiting for transfers between devices: 947 us -> 896 us
  matrix products: 110 us -> 126 us
    all_gather x2, waiting for transfers between devices: 77.2 us -> 26.8 us  [body(): lax.all_gather(values_now, 'seq', axis=0, tiled=True)]
    all_to_all x0 -> x2, waiting for transfers between devices: none -> 48.6 us  [body(): lax.all_to_all(jnp.stack([values_now] * lax.axis_size('seq')), 'seq', 0, 0)]
    all_gather x2, waiting for transfers between devices: 84.7 us -> 39.9 us  [body(): lax.all_gather(keys_now, 'seq', axis=0, tiled=True)]
    dynamic_slice x4 -> x16, local copies, waits for them, and re-layouts: 4.74 us -> 19.2 us  [inner_step(): lax.dynamic_slice_in_dim(value_piece, offset, step_len, 0)]
    unnamed x241 -> x273, local copies, waits for them, and re-layouts: 47.1 us -> 41.5 us
  transfers between devices with their start and end apart: 16 -> 18, of which waited for: 16 -> 15; matrix products, arithmetic and copies ran while one was open for 13% -> 18% of each run, Pallas kernels for 0% -> 0%
where the time goes in v1:
time: 1270 us; the launch traced here: 1260 us
  waiting for transfers between devices  896 us (71%)
  matrix products  126 us (10%)
  local copies, waits for them, and re-layouts  103 us (8%)
  blocking collectives  83.5 us (7%)
  other arithmetic  26.7 us (2%)
  between operations  15.8 us (1%)
    reduce_scatter x4, waiting for transfers between devices, body(): lax.psum_scatter(tuple(grad_sums), ('dp', 'seq'), scatter_dimension=0, ti...  422 us
    unnamed x20, waiting for transfers between devices  218 us
    unnamed x2, blocking collectives  83.5 us
    all_gather x1, waiting for transfers between devices, body(): lax.all_gather(shards[11], ('dp', 'seq'), axis=0, tiled=True)  49.3 us
    all_to_all x2, waiting for transfers between devices, body(): lax.all_to_all(jnp.stack([values_now] * lax.axis_size('seq')), 'seq', 0, 0)  48.6 us
    all_gather x1, waiting for transfers between devices, body(): lax.all_gather(shards[9], ('dp', 'seq'), axis=0, tiled=True)  43.1 us
    unnamed x273, local copies, waits for them, and re-layouts  41.5 us
    all_gather x2, waiting for transfers between devices, body(): lax.all_gather(keys_now, 'seq', axis=0, tiled=True)  39.9 us
  transfers between devices with their start and end apart: 18, of which 15 were waited for; matrix products, arithmetic and copies ran while one was open for 18% of the time, Pallas kernels for 0%

profile of v1, /device:TPU:0, one launch (start us, length us, event | category | flops | bytes accessed | tf_op | source)
XLA Modules:
  0.0 1261.6 jit_solution(16376697008124305342)
XLA Ops:
  15.5 42.8 %all-reduce.19 = (bf16[768]{0:T(1024)(128)(2,1)S(1)}, bf16[768]{0:T(1024)(128)(2,1)S(1)}, bf16[768]{0:T(1024)(128)(2,1)S(1)}, bf16[768]{0:T(1024)(128)(2,1)S(1)}...) all-reduce(bf16[768]{0:T(1024)(128)(2,1)S(1)} %dynamic-update-slice, ...), channel_id=1, replica_groups=mesh['dp'=4,'seq'=8] {'dp','seq'}, use_global_device_ids=true, to_apply=%add.1 | all-reduce | flops 9216 | bytes 36864
  60.8 12.9 %all-gather.9.cloned.1.call-done = bf16[768,2304]{1,0:T(8,128)(2,1)} async-done(((bf16[24,2304]{1,0:T(8,128)(2,1)}), bf16[768,2304]{1,0:T(8,128)(2,1)}) %all-gather.9.cloned.1.call-update) | async-done | bytes 3538960 | tf_op jit(solution)/shard_map/all_gather | solution.py:188
  85.0 4.4 all-to-all-start.1
  93.8 48.5 %all-to-all-done.1 = bf16[8,128,768]{1,2,0:T(8,128)(2,1)S(1)} async-done(((bf16[8,128,768]{1,2,0:T(8,128)(2,1)}), bf16[8,128,768]{1,2,0:T(8,128)(2,1)S(1)}, u32[]{:S(2)}, u32[]{:S(2)}) %all-to-all-start.1) | async-done | bytes 1572896 | tf_op jit(solution)/shard_map/all_to_all | solution.py:238
  143.7 4.3 all-to-all-start
  151.6 18.8 %while.81 = (s32[]{:T(128)}, f32[128,12,64]{0,2,1:T(8,128)}, f32[12,128]{1,0:T(8,128)S(1)}, bf16[1024,768]{1,0:T(8,128)(2,1)}, s32[2,2]{0,1:T(2,128)}, /*index=5...) while((s32[]{:T(128)}, f32[128,12,64]{0,2,1:T(8,128)}, ...), condition=%wide.region_15.16_spmd.clone, body=%wide.region_11.0_spmd.clone.sunk | while | flops 206512768 | bytes 14092886 | solution.py:86
  166.9 3.4 fusion.290
  171.8 35.5 %all-gather.13.cloned.1.call-done = bf16[768,768]{1,0:T(8,128)(2,1)} async-done(((bf16[24,768]{1,0:T(8,128)(2,1)}), bf16[768,768]{1,0:T(8,128)(2,1)}) %all-gather.13.cloned.1.call-update) | async-done | bytes 1179664 | tf_op jit(solution)/shard_map/all_gather | solution.py:191
  213.1 39.9 %all-gather.11.cloned.1.call-done = bf16[1024,768]{1,0:T(8,128)(2,1)} async-done(((bf16[128,768]{1,0:T(8,128)(2,1)}), bf16[1024,768]{1,0:T(8,128)(2,1)}) %all-gather.11.cloned.1.call-update) | async-done | bytes 1572880 | tf_op jit(solution)/shard_map/all_gather | solution.py:236
  254.7 16.1 %while.80 = (s32[]{:T(128)}, f32[128,12,64]{0,2,1:T(8,128)}, f32[12,128]{1,0:T(8,128)S(1)}, bf16[1024,768]{1,0:T(8,128)(2,1)}, s32[2,2]{0,1:T(2,128)S(1)}, /*ind...) while((s32[]{:T(128)}, f32[128,12,64]{0,2,1:T(8,128)}, ...), condition=%wide.region_6.7_spmd.clone, body=%wide.region_2.6_spmd.clone.sunk | while | flops 206512768 | bytes 13806110 | solution.py:86
  274.5 43.1 %all-gather.15.cloned.1.call-done = bf16[768,3072]{1,0:T(8,128)(2,1)} async-done(((bf16[24,3072]{1,0:T(8,128)(2,1)}), bf16[768,3072]{1,0:T(8,128)(2,1)}) %all-gather.15.cloned.1.call-update) | async-done | bytes 4718608 | tf_op jit(solution)/shard_map/all_gather | solution.py:195
  317.7 8.7 multiply_convert_fusion
  326.4 6.6 multiply_convert_fusion.1
  333.0 49.3 %all-gather.17.cloned.1.call-done = bf16[3072,768]{1,0:T(8,128)(2,1)} async-done(((bf16[96,768]{1,0:T(8,128)(2,1)}), bf16[3072,768]{1,0:T(8,128)(2,1)}) %all-gather.17.cloned.1.call-update) | async-done | bytes 4718608 | tf_op jit(solution)/shard_map/all_gather | solution.py:197
  382.3 5.8 convert_reduce_fusion
  400.8 26.8 %all-gather.23.cloned.1.call-done = bf16[1024,768]{1,0:T(8,128)(2,1)} async-done(((bf16[128,768]{1,0:T(8,128)(2,1)}), bf16[1024,768]{1,0:T(8,128)(2,1)}) %all-gather.23.cloned.1.call-update) | async-done | bytes 1572880 | tf_op jit(solution)/shard_map/all_gather | solution.py:298
  430.3 36.6 %while.83 = (s32[]{:T(128)}, f32[128,12,64]{0,2,1:T(8,128)}, bf16[1024,768]{0,1:T(8,128)(2,1)}, bf16[1024,768]{0,1:T(8,128)(2,1)}, bf16[1024,768]{0,1:T(8,128)(2...) while((s32[]{:T(128)}, f32[128,12,64]{0,2,1:T(8,128)}, ...), condition=%wide.region_35.36_spmd.clone, body=%wide.region_32.35_spmd.clone.sunk | while | flops 510958720 | bytes 70738792 | solution.py:138
  437.8 3.5 fusion.320
  456.0 3.5 fusion.320
  476.5 36.6 %while.82 = (s32[]{:T(128)}, f32[128,12,64]{0,2,1:T(8,128)}, bf16[1024,768]{0,1:T(8,128)(2,1)}, bf16[1024,768]{0,1:T(8,128)(2,1)}, bf16[1024,768]{0,1:T(8,128)(2...) while((s32[]{:T(128)}, f32[128,12,64]{0,2,1:T(8,128)}, ...), condition=%wide.region_24.25_spmd.clone, body=%wide.region_21.24_spmd.clone.sunk | while | flops 510958720 | bytes 69165880 | solution.py:138
  524.0 15.7 %reduce-scatter.31.cloned.1.call-done = bf16[128,768]{1,0:T(8,128)(2,1)} async-done(((bf16[1024,768]{1,0:T(8,128)(2,1)}), bf16[128,768]{1,0:T(8,128)(2,1)}) %reduce-scatter.31.cloned.1.call-update) | async-done | bytes 196624
  540.8 66.5 %reduce-scatter.29.cloned.1.call-done = bf16[128,768]{1,0:T(8,128)(2,1)} async-done(((bf16[1024,768]{1,0:T(8,128)(2,1)}), bf16[128,768]{1,0:T(8,128)(2,1)}) %reduce-scatter.29.cloned.1.call-update) | async-done | bytes 196624
  608.4 66.6 %reduce-scatter.27.cloned.1.call-done = bf16[128,768]{1,0:T(8,128)(2,1)} async-done(((bf16[1024,768]{1,0:T(8,128)(2,1)}), bf16[128,768]{1,0:T(8,128)(2,1)}) %reduce-scatter.27.cloned.1.call-update) | async-done | bytes 196624
  676.1 66.5 %reduce-scatter.25.cloned.1.call-done = bf16[128,768]{1,0:T(8,128)(2,1)} async-done(((bf16[1024,768]{1,0:T(8,128)(2,1)}), bf16[128,768]{1,0:T(8,128)(2,1)}) %reduce-scatter.25.cloned.1.call-update) | async-done | bytes 196624
  745.1 4.2 convolution_add_fusion
  752.1 5.2 convolution_add_fusion.2
  759.9 5.1 convolution_add_fusion.1
  786.0 40.7 %all-reduce.18 = (f32[768]{0:T(1024)S(1)}, f32[768]{0:T(1024)S(1)}, f32[768]{0:T(1024)S(1)}, f32[768]{0:T(1024)S(1)}, f32[768]{0:T(1024)S(1)}, /*index=5*/f32[76...) all-reduce(f32[768]{0:T(1024)S(1)} %add.789, ...), channel_id=6, replica_groups=mesh['dp'=4,'seq'=8] {'dp','seq'}, use_global_device_ids=true, to_apply=%region_42.43.clone | all-reduce | flops 9216 | bytes 73728
  833.2 14.1 %reduce-scatter.19.cloned.1.call-done = f32[24,768]{1,0:T(8,128)} async-done(((f32[768,768]{1,0:T(8,128)}), f32[24,768]{1,0:T(8,128)}) %reduce-scatter.19.cloned.1.call-update) | async-done | bytes 73744 | tf_op jit(solution)/shard_map/reduce_scatter | solution.py:339
  847.2 124.7 %reduce-scatter.17.cloned.1.call-done = f32[24,2304]{1,0:T(8,128)} async-done(((f32[768,2304]{1,0:T(8,128)}), f32[24,2304]{1,0:T(8,128)}) %reduce-scatter.17.cloned.1.call-update) | async-done | bytes 221200 | tf_op jit(solution)/shard_map/reduce_scatter | solution.py:339
  972.0 141.4 %reduce-scatter.21.cloned.1.call-done = f32[24,3072]{1,0:T(8,128)} async-done(((f32[768,3072]{1,0:T(8,128)}), f32[24,3072]{1,0:T(8,128)}) %reduce-scatter.21.cloned.1.call-update) | async-done | bytes 294928 | tf_op jit(solution)/shard_map/reduce_scatter | solution.py:339
  1113.4 141.5 %reduce-scatter.23.cloned.1.call-done = f32[96,768]{1,0:T(8,128)} async-done(((f32[3072,768]{1,0:T(8,128)}), f32[96,768]{1,0:T(8,128)}) %reduce-scatter.23.cloned.1.call-update) | async-done | bytes 294928 | tf_op jit(solution)/shard_map/reduce_scatter | solution.py:339
  (629 shorter events, 213.7 us)
Async XLA Ops:
  7.2 66.6 %all-gather.9.cloned.1.call-start = ((), (), s32[]{:S(2)}) async-start(), calls=%async_computation.10 | async-start | bytes 3649536 | tf_op jit(solution)/shard_map/all_gather | solution.py:188
  7.9 141.9 %all-gather.19.cloned.1.call-start = ((), (), s32[]{:S(2)}) async-start(), calls=%async_computation.15 | async-start | bytes 1769472 | tf_op jit(solution)/shard_map/all_gather | solution.py:236
  77.3 129.9 %all-gather.13.cloned.1.call-start = ((), (), s32[]{:S(2)}) async-start(), calls=%async_computation.12 | async-start | bytes 1216512 | tf_op jit(solution)/shard_map/all_gather | solution.py:191
  78.0 174.9 %all-gather.11.cloned.1.call-start = ((), (), s32[]{:S(2)}) async-start(), calls=%async_computation.11 | async-start | bytes 1769472 | tf_op jit(solution)/shard_map/all_gather | solution.py:236
  81.6 236.0 %all-gather.15.cloned.1.call-start = ((), (), s32[]{:S(2)}) async-start(), calls=%async_computation.13 | async-start | bytes 4866048 | tf_op jit(solution)/shard_map/all_gather | solution.py:195
  82.2 300.1 %all-gather.17.cloned.1.call-start = ((), (), s32[]{:S(2)}) async-start(), calls=%async_computation.14 | async-start | bytes 4866048 | tf_op jit(solution)/shard_map/all_gather | solution.py:197
  82.8 344.8 %all-gather.23.cloned.1.call-start = ((), (), s32[]{:S(2)}) async-start(), calls=%async_computation.17 | async-start | bytes 1769472 | tf_op jit(solution)/shard_map/all_gather | solution.py:298
  85.0 57.3 %all-to-all-start.1 = ((bf16[8,128,768]{1,2,0:T(8,128)(2,1)}), bf16[8,128,768]{1,2,0:T(8,128)(2,1)S(1)}, u32[]{:S(2)}, u32[]{:S(2)}) async-start(bf16[8,128,768]{1,2,0:T(8,128)(2,1)} %stack.18), calls=%async_computation.1 | async-start | bytes 3145728 | tf_op jit(solution)/shard_map/all_to_all | solution.py:238
  89.5 384.3 %all-gather.21.cloned.1.call-start = ((), (), s32[]{:S(2)}) async-start(), calls=%async_computation.16 | async-start | bytes 1769472 | tf_op jit(solution)/shard_map/all_gather | solution.py:298
  143.7 66.7 %all-to-all-start = ((bf16[8,128,768]{1,2,0:T(8,128)(2,1)}), bf16[8,128,768]{1,2,0:T(8,128)(2,1)}, u32[]{:S(2)}, u32[]{:S(2)}) async-start(bf16[8,128,768]{1,2,0:T(8,128)(2,1)} %stack.16), calls=%async_computation | async-start | bytes 3145728 | tf_op jit(solution)/shard_map/all_to_all | solution.py:238
  148.0 391.6 %reduce-scatter.31.cloned.1.call-start = ((), (), s32[]{:S(2)}) async-start(), calls=%async_computation.25 | async-start | bytes 1769472
  270.8 55.6 %copy-start.4 = (bf16[1024,768]{0,1:T(8,128)(2,1)}, bf16[1024,768]{0,1:T(8,128)(2,1)S(1)}, u32[]{:S(2)}) copy-start(bf16[1024,768]{0,1:T(8,128)(2,1)S(1)} %get-tuple-element.2085) | copy-start | bytes 4718596
  272.4 53.9 %copy-start.63 = (bf16[128,12,64]{0,2,1:T(8,128)(2,1)}, bf16[128,12,64]{0,2,1:T(8,128)(2,1)S(1)}, u32[]{:S(2)}) copy-start(bf16[128,12,64]{0,2,1:T(8,128)(2,1)S(1)} %fusion.136) | copy-start | bytes 589828
  274.2 122.4 %copy-start.18 = (f32[128,768]{1,0:T(8,128)}, f32[128,768]{1,0:T(8,128)S(1)}, u32[]{:S(2)}) copy-start(f32[128,768]{1,0:T(8,128)S(1)} %get-tuple-element.1633) | copy-start | bytes 1179652
  274.2 52.1 %copy-start.100 = (f32[128]{0:T(128)}, f32[128]{0:T(128)S(1)}, u32[]{:S(2)}) copy-start(f32[128]{0:T(128)S(1)} %broadcast_multiply_fusion.2) | copy-start | bytes 1540
  274.4 51.9 %copy-start.135 = (f32[128]{0:T(128)}, f32[128]{0:T(128)S(1)}, u32[]{:S(2)}) copy-start(f32[128]{0:T(128)S(1)} %multiply_reduce_fusion.7) | copy-start | bytes 1540
  326.4 55.9 %copy-start.45 = (bf16[2,1,128,768]{3,2,1,0:T(8,128)(2,1)S(1)}, bf16[2,1,128,768]{3,2,1,0:T(8,128)(2,1)}, u32[]{:S(2)}) copy-start(bf16[2,1,128,768]{3,2,1,0:T(8,128)(2,1)} %param.25) | copy-start | bytes 1179652
  469.6 137.7 %reduce-scatter.29.cloned.1.call-start = ((), (), s32[]{:S(2)}) async-start(), calls=%async_computation.24 | async-start | bytes 1769472
  473.7 201.3 %reduce-scatter.27.cloned.1.call-start = ((), (), s32[]{:S(2)}) async-start(), calls=%async_computation.23 | async-start | bytes 1769472
  515.7 226.9 %reduce-scatter.25.cloned.1.call-start = ((), (), s32[]{:S(2)}) async-start(), calls=%async_computation.22 | async-start | bytes 1769472
  518.7 328.5 %reduce-scatter.19.cloned.1.call-start = ((), (), s32[]{:S(2)}) async-start(), calls=%async_computation.19 | async-start | bytes 2433024 | tf_op jit(solution)/shard_map/reduce_scatter | solution.py:339
  522.0 221.7 %copy-start.10 = (bf16[2,1,128,768]{3,2,1,0:T(8,128)(2,1)S(1)}, bf16[2,1,128,768]{3,2,1,0:T(8,128)(2,1)}, u32[]{:S(2)}) copy-start(bf16[2,1,128,768]{3,2,1,0:T(8,128)(2,1)} %param.24) | copy-start | bytes 1179652
  522.1 221.7 %copy-start.76 = (f32[768]{0:T(1024)S(1)}, f32[768]{0:T(1024)}, u32[]{:S(2)}) copy-start(f32[768]{0:T(1024)} %copy-done.75) | copy-start | bytes 9220
  522.1 221.7 %copy-start.82 = (f32[768]{0:T(1024)S(1)}, f32[768]{0:T(1024)}, u32[]{:S(2)}) copy-start(f32[768]{0:T(1024)} %copy-done.81) | copy-start | bytes 9220
  522.1 221.7 %copy-start.89 = (f32[128]{0:T(128)S(1)}, f32[128]{0:T(128)}, u32[]{:S(2)}) copy-start(f32[128]{0:T(128)} %copy-done.88) | copy-start | bytes 1540
  522.1 221.7 %copy-start.104 = (f32[128]{0:T(128)S(1)}, f32[128]{0:T(128)}, u32[]{:S(2)}) copy-start(f32[128]{0:T(128)} %copy-done.103) | copy-start | bytes 1540
  522.1 449.9 %reduce-scatter.17.cloned.1.call-start = ((), (), s32[]{:S(2)}) async-start(), calls=%async_computation.18 | async-start | bytes 7299072 | tf_op jit(solution)/shard_map/reduce_scatter | solution.py:339
  523.2 221.9 %copy-start.69 = (bf16[128,12,64]{0,2,1:T(8,128)(2,1)}, bf16[128,12,64]{0,2,1:T(8,128)(2,1)S(1)}, u32[]{:S(2)}) copy-start(bf16[128,12,64]{0,2,1:T(8,128)(2,1)S(1)} %get-tuple-element.1579) | copy-start | bytes 589828
  524.0 221.0 %copy-start.73 = (bf16[128,12,64]{0,2,1:T(8,128)(2,1)}, bf16[128,12,64]{0,2,1:T(8,128)(2,1)S(1)}, u32[]{:S(2)}) copy-start(bf16[128,12,64]{0,2,1:T(8,128)(2,1)S(1)} %get-tuple-element.1581) | copy-start | bytes 589828
  608.4 136.7 %copy-start.67 = (bf16[128,768]{0,1:T(8,128)(2,1)}, bf16[128,768]{0,1:T(8,128)(2,1)S(1)}, u32[]{:S(2)}) copy-start(bf16[128,768]{0,1:T(8,128)(2,1)S(1)} %copy.186) | copy-start | bytes 589828
  749.3 364.0 %reduce-scatter.21.cloned.1.call-start = ((), (), s32[]{:S(2)}) async-start(), calls=%async_computation.20 | async-start | bytes 9732096 | tf_op jit(solution)/shard_map/reduce_scatter | solution.py:339
  757.2 497.6 %reduce-scatter.23.cloned.1.call-start = ((), (), s32[]{:S(2)}) async-start(), calls=%async_computation.21 | async-start | bytes 9732096 | tf_op jit(solution)/shard_map/reduce_scatter | solution.py:339
  (147 other events, 1083.3 us)
Sparse Core Ops, SparseCore 0:
  10.9 62.8 all-gather.8
  77.4 63.7 all-gather.18
  144.2 63.0 all-gather.12
  209.8 43.0 all-gather.10
  255.7 61.8 all-gather.14
  320.4 61.8 all-gather.16
  385.0 42.5 all-gather.22
  429.8 42.5 all-gather.20
  475.8 63.8 reduce-scatter.30
  543.0 64.2 reduce-scatter.28
  610.7 64.2 reduce-scatter.26
  678.3 64.2 reduce-scatter.24
  748.5 98.7 reduce-scatter.18
  853.4 118.5 reduce-scatter.16
  978.3 135.0 reduce-scatter.20
  1119.7 135.1 reduce-scatter.22
